TPU v7x, 128 devices: a whole 4x4x4 slice. The times are simulated.
128 devices in a mesh: grp: 2 (over y_hi), row: 64 (over z, y_lo, x, core).
Axes of the slice: x: 4, y: 4 (y_hi: 2, y_lo: 2; y = y_hi * 2 + y_lo), z: 4, core: 2. Of those that a mesh axis runs over, the one named last changes fastest.
Arguments:
- features: bfloat16 [65536, 256], P(('grp', 'row')), may hold values from -6 to 6
- weight: bfloat16 [256, 256], replicated, may hold values from -0.375 to 0.375
- block_vals: bfloat16 [2, 512, 16, 128, 128], P('grp', 'row'), may hold values from -0.125 to 0.125
- block_cols: int32 [2, 512, 16], P('grp', 'row'), may hold values from 0 to 255, as said below
- block_count: int32 [2, 512], P('grp', 'row'), may hold values from 1 to 16, as said below
- cotangent: bfloat16 [65536, 256], P(('grp', 'row')), may hold values from -6 to 6
Outputs:
- activated: bfloat16 [65536, 256], P(('grp', 'row'))
- weight_grad: float32 [256, 256], replicated
- input_grad: bfloat16 [65536, 256], P(('grp', 'row'))
Inputs may be any that keep to these rules, and one draw needn't show every extreme that they name: `block_cols`: within one destination row block the 16 column blocks are distinct and ascending. `block_count`: in every draw some device holds 16 live slots in each of its row blocks.
All inputs are finite; a program needn't handle non-finite values.
Results may differ from a plain program's by a relative error of at most 0.0062.
Values may be sent and summed in bfloat16 or wider, within the bound.
No kernel may reach another device: no remote copies, remote signals or barrier semaphores. Data moves between devices by JAX's collectives and lax.ppermute only.
A program may use at most 128 MiB of HBM per device.

v0:
```python
import math
import jax
import jax.numpy as jnp
from jax import lax
from jax.sharding import PartitionSpec as P


def silu_slope(pre):
    sigma = jax.nn.sigmoid(pre)
    return sigma * (1.0 + pre * (1.0 - sigma))


def body(features, weight, block_vals, block_cols, block_count, cotangent):
    rows_dev, width = features.shape
    block = block_vals.shape[-1]
    slot_total = block_vals.shape[2]
    groups = lax.axis_size("grp")
    members = lax.axis_size("row")
    verts = rows_dev * groups * members
    slots = jnp.arange(slot_total)
    gathered = lax.all_gather(features, "row", axis=0, tiled=True)
    col_blocks = gathered.shape[0] // block
    panel_blocks = gathered.reshape(col_blocks, block, width)

    def aggregate(items):
        values, columns, count = items
        masked = jnp.where((slots < count)[:, None, None], values, jnp.zeros_like(values))
        picked = panel_blocks[columns]
        return jnp.einsum("kij,kjf->if", masked, picked, preferred_element_type=jnp.float32)

    partial_value = lax.map(aggregate, (block_vals[0], block_cols[0], block_count[0])).reshape(
        -1, width
    )
    summed = lax.psum_scatter(partial_value, "grp", scatter_dimension=0, tiled=True)
    aggregated = summed.astype(jnp.bfloat16)
    pre = jnp.dot(aggregated, weight, preferred_element_type=jnp.float32)
    activated = jax.nn.silu(pre).astype(jnp.bfloat16)
    pre_grad = (cotangent.astype(jnp.float32) * silu_slope(pre)).astype(jnp.bfloat16)
    local_grad = jnp.dot(aggregated.T, pre_grad, preferred_element_type=jnp.float32)
    own_grad = jnp.dot(pre_grad, weight.T, preferred_element_type=jnp.float32).astype(jnp.bfloat16)
    rows_grad = lax.all_gather(own_grad, "grp", axis=0, tiled=True)
    weight_grad = lax.psum(local_grad, ("grp", "row")) * (1.0 / math.sqrt(verts))
    by_block = rows_grad.reshape(-1, block, width)

    def spread(carry, items):
        values, columns, count, grad_block = items
        masked = jnp.where((slots < count)[:, None, None], values, jnp.zeros_like(values))
        contrib = jnp.einsum("kij,if->kjf", masked, grad_block, preferred_element_type=jnp.float32)
        return (carry.at[columns].add(contrib), None)

    total, unused = lax.scan(
        spread,
        jnp.zeros((col_blocks, block, width), jnp.float32),
        (block_vals[0], block_cols[0], block_count[0], by_block),
    )
    term = total.reshape(-1, width)
    input_grad = lax.psum_scatter(term, "row", scatter_dimension=0, tiled=True).astype(jnp.bfloat16)
    return (activated, weight_grad, input_grad)


def solution(mesh):
    placed = (
        P(("grp", "row"), None),
        P(),
        P("grp", "row", None, None, None),
        P("grp", "row", None),
        P("grp", "row"),
        P(("grp", "row"), None),
    )
    return jax.shard_map(
        body,
        mesh=mesh,
        in_specs=placed,
        out_specs=(P(("grp", "row"), None), P(), P(("grp", "row"), None)),
        check_vma=False,
    )
```

profile of v0, /device:TPU:0, one launch (start us, length us, event | category | flops | bytes accessed | tf_op | source)
XLA Modules:
  0.0 743.3 jit_solution(15940612499893916046)
XLA Ops:
  8.0 127.3 %all-gather.2.cloned.1.call-done = bf16[32768,256]{1,0:T(8,128)(2,1)} async-done(((bf16[512,256]{1,0:T(8,128)(2,1)}), bf16[32768,256]{1,0:T(8,128)(2,1)}) %all-gather.2.cloned.1.call-update) | async-done | bytes 16777232 | tf_op jit(solution)/shard_map/all_gather | solution.py:21
  135.3 88.4 %while.22 = (s32[]{:T(128)}, f32[8,128,256]{2,1,0:T(8,128)}, s32[8]{0:T(128)}, bf16[8,16,128,128]{3,2,1,0:T(8,128)(2,1)}, s32[8,16]{1,0:T(8,128)}, /*index=5*/bf16[256,128,256]{2,1,0:T(8,128)(2,1)}, s32[]{:T(128)}) while((s32[]{:T(128)}, f32[8,128,256]{2,1,0:T(8,128)}, s32[8]{0:T(128)}, bf16[8,16,128,128]{3,2,1,0:T(8,128)(2,1)}, ...), condition=%wide.region_1.2_spmd.clone, body=%wide.region_0.1_spmd.clone.sunk | while | flops 134480960 | bytes 3806601 | solution.py:31
  137.9 6.4 gather_fusion
  148.9 6.4 gather_fusion
  160.0 6.4 gather_fusion
  171.0 6.4 gather_fusion
  182.1 6.4 gather_fusion
  193.1 6.4 gather_fusion
  204.1 6.4 gather_fusion
  215.2 6.4 gather_fusion
  223.7 6.5 copy.9
  230.2 17.2 %reduce-scatter.3.cloned.1.call-done = f32[512,256]{1,0:T(8,128)} async-done(((f32[1024,256]{1,0:T(8,128)}), f32[512,256]{1,0:T(8,128)}) %reduce-scatter.3.cloned.1.call-update) | async-done | bytes 524304 | tf_op jit(solution)/shard_map/reduce_scatter | solution.py:34
  250.9 10.2 %all_gather.7 = bf16[1024,256]{1,0:T(8,128)(2,1)S(1)} all-gather(bf16[512,256]{1,0:T(8,128)(2,1)S(1)} %convolution_convert_fusion), channel_id=1, replica_groups=mesh['grp'=2,'row'=64] {'grp'}, dimensions={0}, use_global_device_ids=true | all-gather | bytes 786432 | tf_op jit(solution)/shard_map/all_gather | solution.py:41
  261.1 11.2 %broadcast_in_dim.28 = f32[256,128,256]{2,1,0:T(8,128)} broadcast(f32[]{:T(128)} %constant.27.clone.1), dimensions={} | broadcast | bytes 33554436 | tf_op jit(solution)/shard_map/broadcast_in_dim | solution.py:53
  272.4 63.8 %while.23 = (s32[]{:T(128)}, f32[256,128,256]{2,1,0:T(8,128)}, s32[8,16]{1,0:T(8,128)}, s32[8]{0:T(128)S(1)}, bf16[8,16,128,128]{2,3,1,0:T(8,128)(2,1)}, /*index=5*/bf16[8,128,256]{2,1,0:T(8,128)(2,1)S(1)}, s32[]{:T(128)}) while((s32[]{:T(128)}, f32[256,128,256]{2,1,0:T(8,128)}, s32[8,16]{1,0:T(8,128)}, s32[8]{0:T(128)S(1)}, ...), condition=%wide.region_6.7_spmd.clone, body=%wide.region_4.6_spmd.clone.sunk | while | flops 135004224 | bytes 8980281 | solution.py:51
  275.7 4.6 scatter_fusion
  283.7 4.6 scatter_fusion
  299.7 4.6 scatter_fusion
  307.7 4.6 scatter_fusion
  315.7 4.6 scatter_fusion
  323.6 4.6 scatter_fusion
  331.6 4.6 scatter_fusion
  336.2 58.5 %all-reduce.2.cloned.1.call-done = f32[256,256]{1,0:T(8,128)} async-done(((f32[256,256]{1,0:T(8,128)}), f32[256,256]{1,0:T(8,128)}) %all-reduce.2.cloned.1.call-update) | async-done | bytes 262160 | tf_op jit(solution)/shard_map/psum | solution.py:42
  396.5 338.6 %reduce-scatter.5.cloned.1.call-done = f32[512,256]{1,0:T(8,128)} async-done(((f32[32768,256]{1,0:T(8,128)}), f32[512,256]{1,0:T(8,128)}) %reduce-scatter.5.cloned.1.call-update) | async-done | bytes 524304 | tf_op jit(solution)/shard_map/reduce_scatter | solution.py:57
  (95 shorter events, 76.4 us)
Async XLA Ops:
  7.2 240.2 %copy-start = (bf16[256,256]{1,0:T(8,128)(2,1)S(1)}, bf16[256,256]{1,0:T(8,128)(2,1)}, u32[]{:S(2)}) copy-start(bf16[256,256]{1,0:T(8,128)(2,1)} %param.11) | copy-start | bytes 393220
  7.2 128.1 %all-gather.2.cloned.1.call-start = ((), (), s32[]{:S(2)}) async-start(), calls=%async_computation.2 | async-start | bytes 17039360 | tf_op jit(solution)/shard_map/all_gather | solution.py:21
  7.9 239.5 %reduce-scatter.3.cloned.1.call-start = ((), (), s32[]{:S(2)}) async-start(), calls=%async_computation.3 | async-start | bytes 1572864 | tf_op jit(solution)/shard_map/reduce_scatter | solution.py:34
  223.7 23.7 %copy-start.2 = (bf16[512,256]{1,0:T(8,128)(2,1)S(1)}, bf16[512,256]{1,0:T(8,128)(2,1)}, u32[]{:S(2)}) copy-start(bf16[512,256]{1,0:T(8,128)(2,1)} %param.15) | copy-start | bytes 786436
  223.7 171.1 %all-reduce.2.cloned.1.call-start = ((), (), s32[]{:S(2)}) async-start(), calls=%async_computation.4 | async-start | bytes 524288 | tf_op jit(solution)/shard_map/psum | solution.py:42
  247.4 2.5 copy-start.1
  250.9 484.1 %reduce-scatter.5.cloned.1.call-start = ((), (), s32[]{:S(2)}) async-start(), calls=%async_computation.5 | async-start | bytes 34078720 | tf_op jit(solution)/shard_map/reduce_scatter | solution.py:57
  261.1 11.2 %copy-start.3 = (s32[8]{0:T(128)S(1)}, s32[8]{0:T(128)}, u32[]{:S(2)}) copy-start(s32[8]{0:T(128)} %get-tuple-element.273) | copy-start | bytes 100
Sparse Core Ops, SparseCore 0:
  9.7 125.4 all-gather.1
  223.8 23.5 reduce-scatter.2
  253.4 141.3 all-reduce.1
  397.2 337.8 reduce-scatter.4
where the time goes:
time: 746 us; the launch traced here: 743 us
  waiting for transfers between devices  542 us (73%)
  local copies, waits for them, and re-layouts  83.3 us (11%)
  other arithmetic  61.3 us (8%)
  matrix products  32 us (4%)
  between operations  13.8 us (2%)
  blocking collectives  10.2 us (1%)
    reduce_scatter x1, waiting for transfers between devices, body(): lax.psum_scatter(term, 'row', scatter_dimension=0, tiled=True)  339 us
    all_gather x1, waiting for transfers between devices, body(): gathered = lax.all_gather(features, 'row', axis=0, tiled=True)  127 us
    psum x1, waiting for transfers between devices, body(): lax.psum(local_grad, ('grp', 'row')) * (1.0 / math.sqrt(verts))  58.5 us
    gather x8, local copies, waits for them, and re-layouts, aggregate(): picked = panel_blocks[columns]  51.1 us
    scatter-add x8, other arithmetic, spread(): return (carry.at[columns].add(contrib), None)  36.9 us
    reduce_scatter x1, waiting for transfers between devices, body(): lax.psum_scatter(partial_value, 'grp', scatter_dimension=0, tiled=True)  17.2 us
    dot_general x8, matrix products, aggregate(): jnp.einsum('kij,kjf->if', masked, picked, preferred_element_type=jnp.floa...  16.4 us
  transfers between devices with their start and end apart: 4, of which 4 were waited for; matrix products, arithmetic and copies ran while one was open for 11% of the time, Pallas kernels for 0%

commit v1 on v0

--- a/solution.py
+++ b/solution.py
@@ -3,6 +3,7 @@
 import jax.numpy as jnp
 from jax import lax
 from jax.sharding import PartitionSpec as P
+from jax.lax import psum
 
 
 def silu_slope(pre):
@@ -39,7 +40,9 @@
     local_grad = jnp.dot(aggregated.T, pre_grad, preferred_element_type=jnp.float32)
     own_grad = jnp.dot(pre_grad, weight.T, preferred_element_type=jnp.float32).astype(jnp.bfloat16)
     rows_grad = lax.all_gather(own_grad, "grp", axis=0, tiled=True)
-    weight_grad = lax.psum(local_grad, ("grp", "row")) * (1.0 / math.sqrt(verts))
+    weight_grad = psum(psum(local_grad, axis_name="row"), axis_name="grp") * (
+        1.0 / math.sqrt(verts)
+    )
     by_block = rows_grad.reshape(-1, block, width)
 
     def spread(carry, items):

time: 746 us -> 1180 us (1.58)
  waiting for transfers between devices: 542 us -> 973 us
    psum x1 -> x2, waiting for transfers between devices: 58.5 us -> 491 us  [the longest x1 491 us: body(): psum(local_grad, axis_name='row')]
  transfers between devices with their start and end apart: 4 -> 5, of which waited for: 4 -> 4; matrix products, arithmetic and copies ran while one was open for 11% -> 7% of each run, Pallas kernels for 0% -> 0%
where the time goes in v1:
time: 1180 us
  waiting for transfers between devices  973 us (82%)
  local copies, waits for them, and re-layouts  83.3 us (7%)
  other arithmetic  62 us (5%)
  matrix products  33 us (3%)
  between operations  13.8 us (1%)
    psum x1, waiting for transfers between devices, body(): psum(local_grad, axis_name='row')  491 us
    reduce_scatter x1, waiting for transfers between devices, body(): lax.psum_scatter(term, 'row', scatter_dimension=0, tiled=True)  337 us
    all_gather x1, waiting for transfers between devices, body(): gathered = lax.all_gather(features, 'row', axis=0, tiled=True)  127 us
    gather x8, local copies, waits for them, and re-layouts, aggregate(): picked = panel_blocks[columns]  51.1 us
    scatter-add x8, other arithmetic, spread(): return (carry.at[columns].add(contrib), None)  36.9 us
  transfers between devices with their start and end apart: 5, of which 4 were waited for; matrix products, arithmetic and copies ran while one was open for 7% of the time, Pallas kernels for 0%

profile of v1, /device:TPU:0, one launch (start us, length us, event | category | flops | bytes accessed | tf_op | source)
XLA Modules:
  0.0 1175.7 jit_solution(8273087130929243374)
XLA Ops:
  8.0 127.3 %all-gather.2.cloned.1.call-done = bf16[32768,256]{1,0:T(8,128)(2,1)} async-done(((bf16[512,256]{1,0:T(8,128)(2,1)}), bf16[32768,256]{1,0:T(8,128)(2,1)}) %all-gather.2.cloned.1.call-update) | async-done | bytes 16777232 | tf_op jit(solution)/shard_map/all_gather | solution.py:22
  135.3 88.4 %while.22 = (s32[]{:T(128)}, f32[8,128,256]{2,1,0:T(8,128)}, s32[8]{0:T(128)}, bf16[8,16,128,128]{3,2,1,0:T(8,128)(2,1)}, s32[8,16]{1,0:T(8,128)}, /*index=5*/bf16[256,128,256]{2,1,0:T(8,128)(2,1)}, s32[]{:T(128)}) while((s32[]{:T(128)}, f32[8,128,256]{2,1,0:T(8,128)}, s32[8]{0:T(128)}, bf16[8,16,128,128]{3,2,1,0:T(8,128)(2,1)}, ...), condition=%wide.region_1.2_spmd.clone, body=%wide.region_0.1_spmd.clone.sunk | while | flops 134480960 | bytes 3806601 | solution.py:32
  137.9 6.4 gather_fusion
  148.9 6.4 gather_fusion
  160.0 6.4 gather_fusion
  171.0 6.4 gather_fusion
  182.1 6.4 gather_fusion
  193.1 6.4 gather_fusion
  204.1 6.4 gather_fusion
  215.2 6.4 gather_fusion
  223.7 6.5 copy.9
  230.2 17.2 %reduce-scatter.3.cloned.1.call-done = f32[512,256]{1,0:T(8,128)} async-done(((f32[1024,256]{1,0:T(8,128)}), f32[512,256]{1,0:T(8,128)}) %reduce-scatter.3.cloned.1.call-update) | async-done | bytes 524304 | tf_op jit(solution)/shard_map/reduce_scatter | solution.py:35
  251.9 10.2 all_gather.7
  262.1 491.0 %all-reduce.3.cloned.1.call-done = f32[256,256]{1,0:T(8,128)} async-done(((f32[256,256]{1,0:T(8,128)}), f32[256,256]{1,0:T(8,128)}) %all-reduce.3.cloned.1.call-update) | async-done | bytes 262160 | tf_op jit(solution)/shard_map/psum | solution.py:43
  753.2 11.2 broadcast_in_dim.28
  764.4 64.6 %while.23 = (s32[]{:T(128)}, f32[256,128,256]{2,1,0:T(8,128)}, s32[8,16]{1,0:T(8,128)}, s32[8]{0:T(128)S(1)}, bf16[8,16,128,128]{2,3,1,0:T(8,128)(2,1)}, /*index=5*/bf16[8,128,256]{2,1,0:T(8,128)(2,1)S(1)}, s32[]{:T(128)}) while((s32[]{:T(128)}, f32[256,128,256]{2,1,0:T(8,128)}, s32[8,16]{1,0:T(8,128)}, s32[8]{0:T(128)S(1)}, ...), condition=%wide.region_7.8_spmd.clone, body=%wide.region_5.7_spmd.clone.sunk | while | flops 135004224 | bytes 8980281 | solution.py:54
  767.9 4.6 scatter_fusion
  775.9 4.7 scatter_fusion
  792.1 4.6 scatter_fusion
  800.2 4.6 scatter_fusion
  808.3 4.6 scatter_fusion
  816.3 4.6 scatter_fusion
  824.4 4.6 scatter_fusion
  830.7 336.6 %reduce-scatter.5.cloned.1.call-done = f32[512,256]{1,0:T(8,128)} async-done(((f32[32768,256]{1,0:T(8,128)}), f32[512,256]{1,0:T(8,128)}) %reduce-scatter.5.cloned.1.call-update) | async-done | bytes 524304 | tf_op jit(solution)/shard_map/reduce_scatter | solution.py:60
  (98 shorter events, 78.2 us)
Async XLA Ops:
  7.2 240.2 %copy-start = (bf16[256,256]{1,0:T(8,128)(2,1)S(1)}, bf16[256,256]{1,0:T(8,128)(2,1)}, u32[]{:S(2)}) copy-start(bf16[256,256]{1,0:T(8,128)(2,1)} %param.11) | copy-start | bytes 393220
  7.2 128.1 %all-gather.2.cloned.1.call-start = ((), (), s32[]{:S(2)}) async-start(), calls=%async_computation.2 | async-start | bytes 17039360 | tf_op jit(solution)/shard_map/all_gather | solution.py:22
  7.9 239.5 %reduce-scatter.3.cloned.1.call-start = ((), (), s32[]{:S(2)}) async-start(), calls=%async_computation.3 | async-start | bytes 1572864 | tf_op jit(solution)/shard_map/reduce_scatter | solution.py:35
  223.7 23.7 %copy-start.2 = (bf16[512,256]{1,0:T(8,128)(2,1)S(1)}, bf16[512,256]{1,0:T(8,128)(2,1)}, u32[]{:S(2)}) copy-start(bf16[512,256]{1,0:T(8,128)(2,1)} %param.15) | copy-start | bytes 786436
  223.7 529.4 %all-reduce.3.cloned.1.call-start = ((), (), s32[]{:S(2)}) async-start(), calls=%async_computation.4 | async-start | bytes 524288 | tf_op jit(solution)/shard_map/psum | solution.py:43
  251.6 577.5 %all-reduce.5.cloned.1.call-start = ((), (), s32[]{:S(2)}) async-start(), calls=%async_computation.5 | async-start | bytes 524288 | tf_op jit(solution)/shard_map/psum | solution.py:43
  753.1 414.3 %reduce-scatter.5.cloned.1.call-start = ((), (), s32[]{:S(2)}) async-start(), calls=%async_computation.6 | async-start | bytes 34078720 | tf_op jit(solution)/shard_map/reduce_scatter | solution.py:60
  753.2 11.2 copy-start.3
  829.0 340.1 %copy-start.1 = (bf16[256,256]{1,0:T(8,128)(2,1)S(1)}, bf16[256,256]{1,0:T(8,128)(2,1)}, u32[]{:S(2)}) copy-start(bf16[256,256]{1,0:T(8,128)(2,1)} %param.11) | copy-start | bytes 393220
Sparse Core Ops, SparseCore 0:
  9.7 125.4 all-gather.1
  223.8 23.5 reduce-scatter.2
  251.7 501.3 all-reduce.2
  755.4 28.5 all-reduce.4
  829.1 338.1 reduce-scatter.4

commit v2 on v0

--- a/solution.py
+++ b/solution.py
@@ -3,6 +3,7 @@
 import jax.numpy as jnp
 from jax import lax
 from jax.sharding import PartitionSpec as P
+from jax.lax import all_gather
 
 
 def silu_slope(pre):
@@ -39,7 +40,7 @@
     local_grad = jnp.dot(aggregated.T, pre_grad, preferred_element_type=jnp.float32)
     own_grad = jnp.dot(pre_grad, weight.T, preferred_element_type=jnp.float32).astype(jnp.bfloat16)
     rows_grad = lax.all_gather(own_grad, "grp", axis=0, tiled=True)
-    weight_grad = lax.psum(local_grad, ("grp", "row")) * (1.0 / math.sqrt(verts))
+    weight_grad = jnp.sum(all_gather(local_grad, ("grp", "row")), axis=0) * (1.0 / math.sqrt(verts))
     by_block = rows_grad.reshape(-1, block, width)
 
     def spread(carry, items):

time: 746 us -> 845 us (1.13)
  waiting for transfers between devices: 542 us -> 625 us
  other arithmetic: 61.3 us -> 73.5 us
    all_gather x0 -> x1, waiting for transfers between devices: none -> 144 us  [body(): all_gather(local_grad, ('grp', 'row'))]
    psum x1 -> x0, waiting for transfers between devices: 58.5 us -> none  [body(): lax.psum(local_grad, ('grp', 'row')) * (1.0 / math.sqrt(verts))]
    reduce_sum x0 -> x1, other arithmetic: none -> 12.2 us  [body(): jnp.sum(all_gather(local_grad, ('grp', 'row')), axis=0)]
    reduce_scatter x1, waiting for transfers between devices: 339 us -> 329 us  [body(): lax.psum_scatter(term, 'row', scatter_dimension=0, tiled=True)]
where the time goes in v2:
time: 845 us; the launch traced here: 843 us
  waiting for transfers between devices  625 us (74%)
  local copies, waits for them, and re-layouts  83.6 us (10%)
  other arithmetic  73.5 us (9%)
  matrix products  33 us (4%)
  blocking collectives  13.8 us (2%)
  between operations  13.8 us (2%)
    reduce_scatter x1, waiting for transfers between devices, body(): lax.psum_scatter(term, 'row', scatter_dimension=0, tiled=True)  329 us
    all_gather x1, waiting for transfers between devices, body(): all_gather(local_grad, ('grp', 'row'))  144 us
    all_gather x1, waiting for transfers between devices, body(): gathered = lax.all_gather(features, 'row', axis=0, tiled=True)  127 us
    gather x8, local copies, waits for them, and re-layouts, aggregate(): picked = panel_blocks[columns]  51.1 us
    scatter-add x8, other arithmetic, spread(): return (carry.at[columns].add(contrib), None)  37.2 us
    reduce_scatter x1, waiting for transfers between devices, body(): lax.psum_scatter(partial_value, 'grp', scatter_dimension=0, tiled=True)  23.6 us
  transfers between devices with their start and end apart: 4, of which 4 were waited for; matrix products, arithmetic and copies ran while one was open for 11% of the time, Pallas kernels for 0%

profile of v2, /device:TPU:0, one launch (start us, length us, event | category | flops | bytes accessed | tf_op | source)
XLA Modules:
  0.0 842.7 jit_solution(5266381408285104476)
XLA Ops:
  8.0 127.3 %all-gather.4.cloned.1.call-done = bf16[32768,256]{1,0:T(8,128)(2,1)} async-done(((bf16[512,256]{1,0:T(8,128)(2,1)}), bf16[32768,256]{1,0:T(8,128)(2,1)}) %all-gather.4.cloned.1.call-update) | async-done | bytes 16777232 | tf_op jit(solution)/shard_map/all_gather | solution.py:22
  135.3 88.4 %while.22 = (s32[]{:T(128)}, f32[8,128,256]{2,1,0:T(8,128)}, s32[8]{0:T(128)}, bf16[8,16,128,128]{3,2,1,0:T(8,128)(2,1)}, s32[8,16]{1,0:T(8,128)}, /*index=5*/bf16[256,128,256]{2,1,0:T(8,128)(2,1)}, s32[]{:T(128)}) while((s32[]{:T(128)}, f32[8,128,256]{2,1,0:T(8,128)}, s32[8]{0:T(128)}, bf16[8,16,128,128]{3,2,1,0:T(8,128)(2,1)}, ...), condition=%wide.region_1.2_spmd.clone, body=%wide.region_0.1_spmd.clone.sunk | while | flops 134480960 | bytes 3806601 | solution.py:32
  137.9 6.4 gather_fusion
  149.0 6.4 gather_fusion
  160.0 6.4 gather_fusion
  171.1 6.4 gather_fusion
  182.1 6.4 gather_fusion
  193.1 6.4 gather_fusion
  204.2 6.4 gather_fusion
  215.2 6.4 gather_fusion
  223.8 23.6 %reduce-scatter.3.cloned.1.call-done = f32[512,256]{1,0:T(8,128)} async-done(((f32[1024,256]{1,0:T(8,128)}), f32[512,256]{1,0:T(8,128)}) %reduce-scatter.3.cloned.1.call-update) | async-done | bytes 524304 | tf_op jit(solution)/shard_map/reduce_scatter | solution.py:35
  251.6 6.5 copy.9
  258.4 13.8 %all_gather.15 = bf16[1024,256]{1,0:T(8,128)(2,1)S(1)} all-gather(bf16[512,256]{1,0:T(8,128)(2,1)S(1)} %convolution_convert_fusion), channel_id=1, replica_groups=mesh['grp'=2,'row'=64] {'grp'}, dimensions={0}, use_global_device_ids=true | all-gather | bytes 786432 | tf_op jit(solution)/shard_map/all_gather | solution.py:42
  272.2 11.3 %broadcast_in_dim.28 = f32[256,128,256]{2,1,0:T(8,128)} broadcast(f32[]{:T(128)} %constant.27.clone.1), dimensions={} | broadcast | bytes 33554436 | tf_op jit(solution)/shard_map/broadcast_in_dim | solution.py:54
  283.5 65.0 %while.23 = (s32[]{:T(128)}, f32[256,128,256]{2,1,0:T(8,128)}, s32[8,16]{1,0:T(8,128)}, s32[8]{0:T(128)S(1)}, bf16[8,16,128,128]{2,3,1,0:T(8,128)(2,1)}, /*index=5*/bf16[8,128,256]{2,1,0:T(8,128)(2,1)S(1)}, s32[]{:T(128)}) while((s32[]{:T(128)}, f32[256,128,256]{2,1,0:T(8,128)}, s32[8,16]{1,0:T(8,128)}, s32[8]{0:T(128)S(1)}, ...), condition=%wide.region_6.7_spmd.clone, body=%wide.region_4.6_spmd.clone.sunk | while | flops 135004224 | bytes 8980281 | solution.py:52
  287.0 4.6 scatter_fusion
  311.2 4.7 scatter_fusion
  319.4 4.7 scatter_fusion
  327.6 4.6 scatter_fusion
  335.7 4.6 scatter_fusion
  343.8 4.7 scatter_fusion
  348.5 144.3 %all-gather.6.cloned.1.call-done = f32[32768,256]{1,0:T(8,128)} async-done(((f32[256,256]{1,0:T(8,128)}), f32[32768,256]{1,0:T(8,128)}) %all-gather.6.cloned.1.call-update) | async-done | bytes 33554448 | tf_op jit(solution)/shard_map/all_gather | solution.py:43
  492.9 12.2 %reduce_sum.9 = f32[256,256]{1,0:T(8,128)S(1)} reduce(f32[128,256,256]{2,1,0:T(8,128)} %bitcast.70, f32[]{:T(128)} %constant.27.clone.1), dimensions={0}, to_apply=%region_3.4 | reduce | flops 8323072 | bytes 33816580 | tf_op jit(solution)/shard_map/reduce_sum | solution.py:43
  505.8 328.6 %reduce-scatter.5.cloned.1.call-done = f32[512,256]{1,0:T(8,128)} async-done(((f32[32768,256]{1,0:T(8,128)}), f32[512,256]{1,0:T(8,128)}) %reduce-scatter.5.cloned.1.call-update) | async-done | bytes 524304 | tf_op jit(solution)/shard_map/reduce_scatter | solution.py:58
  (96 shorter events, 82.0 us)
Async XLA Ops:
  7.2 240.2 %copy-start = (bf16[256,256]{1,0:T(8,128)(2,1)S(1)}, bf16[256,256]{1,0:T(8,128)(2,1)}, u32[]{:S(2)}) copy-start(bf16[256,256]{1,0:T(8,128)(2,1)} %param.11) | copy-start | bytes 393220
  7.2 128.1 %all-gather.4.cloned.1.call-start = ((), (), s32[]{:S(2)}) async-start(), calls=%async_computation.2 | async-start | bytes 17039360 | tf_op jit(solution)/shard_map/all_gather | solution.py:22
  7.9 239.5 %reduce-scatter.3.cloned.1.call-start = ((), (), s32[]{:S(2)}) async-start(), calls=%async_computation.3 | async-start | bytes 1572864 | tf_op jit(solution)/shard_map/reduce_scatter | solution.py:35
  135.3 112.1 %copy-start.2 = (bf16[512,256]{1,0:T(8,128)(2,1)S(1)}, bf16[512,256]{1,0:T(8,128)(2,1)}, u32[]{:S(2)}) copy-start(bf16[512,256]{1,0:T(8,128)(2,1)} %param.15) | copy-start | bytes 786436
  223.7 269.1 %all-gather.6.cloned.1.call-start = ((), (), s32[]{:S(2)}) async-start(), calls=%async_computation.5 | async-start | bytes 33816576 | tf_op jit(solution)/shard_map/all_gather | solution.py:43
  251.6 582.8 %reduce-scatter.5.cloned.1.call-start = ((), (), s32[]{:S(2)}) async-start(), calls=%async_computation.4 | async-start | bytes 34078720 | tf_op jit(solution)/shard_map/reduce_scatter | solution.py:58
  272.2 11.3 %copy-start.3 = (s32[8]{0:T(128)S(1)}, s32[8]{0:T(128)}, u32[]{:S(2)}) copy-start(s32[8]{0:T(128)} %get-tuple-element.273) | copy-start | bytes 100
  492.9 343.3 %copy-start.1 = (bf16[256,256]{1,0:T(8,128)(2,1)S(1)}, bf16[256,256]{1,0:T(8,128)(2,1)}, u32[]{:S(2)}) copy-start(bf16[256,256]{1,0:T(8,128)(2,1)} %param.11) | copy-start | bytes 393220
Sparse Core Ops, SparseCore 0:
  9.7 125.4 all-gather.3
  223.8 23.5 reduce-scatter.2
  251.7 241.0 all-gather.5
  495.2 339.1 reduce-scatter.4
